TPU v7x, 512 devices: a whole 4x4x16 slice. The times are simulated.
512 devices in a mesh: expert: 64 (over x, y, z_hi, core), dp: 8 (over z_lo).
Axes of the slice: x: 4, y: 4, z: 16 (z_hi: 2, z_lo: 8; z = z_hi * 8 + z_lo), core: 2. Of those that a mesh axis runs over, the one named last changes fastest.
Arguments:
- tokens: bfloat16 [256, 2048], P('dp'), may hold values from -6 to 6
- w_gate: bfloat16 [128, 768, 2048], P('expert', 'dp'), may hold values from -2 to 2
- w_up: bfloat16 [128, 768, 2048], P('expert', 'dp'), may hold values from -2 to 2
- w_down: bfloat16 [128, 768, 2048], P('expert', 'dp'), may hold values from -2 to 2
Outputs:
- cosine: float32 [256, 128, 128], P('expert')
All inputs are finite; a program needn't handle non-finite values.
Results may differ from a plain program's by a relative error of at most 0.0014.
Values may be sent and summed in bfloat16 or wider, within the bound.
No kernel may reach another device: no remote copies, remote signals or barrier semaphores. Data moves between devices by JAX's collectives and lax.ppermute only.
A program may use at most 64 MiB of HBM per device.

v0:
```python
import jax
import jax.numpy as jnp
from jax import lax
from jax.sharding import PartitionSpec as P

BOTH = ("expert", "dp")


def z_ring_pairs(mesh, shift):
    axes = mesh.axis_names
    devs = mesh.devices.reshape(-1)
    index_of = {}
    for i, d in enumerate(devs):
        x, y, z = d.coords[:3]
        index_of[x, y, z, d.core_on_chip] = i
    z_len = 1 + max((k[2] for k in index_of))
    pairs = []
    for (x, y, z, c), i in index_of.items():
        pairs.append((i, index_of[x, y, (z + shift) % z_len, c]))
    assert axes == BOTH
    return sorted(pairs)


def gather_blocks(block, rings, n):
    k = lax.axis_index("dp")
    shifts = tuple((s for s, _ in rings))
    received = [block] + [lax.ppermute(block, BOTH, pairs) for _, pairs in rings]
    stacked = jnp.stack(received)
    source = (k - jnp.array((0,) + shifts)) % n
    ordered = jnp.take(stacked, jnp.argsort(source), axis=0)
    return ordered


def doubling_gather(block, n):
    k = lax.axis_index("dp")
    have = block[None]
    codes = [0]
    step = n // 2
    while step:
        pairs = [(i, i ^ step) for i in range(n)]
        have = jnp.concatenate([have, lax.ppermute(have, "dp", pairs)], axis=0)
        codes = codes + [c ^ step for c in codes]
        step //= 2
    where = jnp.array(codes)
    position = jnp.argsort(where)
    return jnp.take(have, position[jnp.arange(n) ^ k], axis=0)


def transpose_blocks(w, n):
    k = lax.axis_index("dp")
    width = w.shape[2] // n
    got = [lax.dynamic_slice_in_dim(w, k * width, width, axis=2)]
    for s in range(1, n):
        piece = lax.dynamic_slice_in_dim(w, (k + s) % n * width, width, axis=2)
        got.append(lax.ppermute(piece, "dp", [(i, (i + s) % n) for i in range(n)]))
    stacked = jnp.stack(got, axis=1)
    source = (k - jnp.arange(n)) % n
    ordered = jnp.take(stacked, jnp.argsort(source), axis=1)
    return ordered.reshape(w.shape[0], -1, width)


def all_reduce_dp(x, n):
    pieces = x.reshape((n, -1))
    mine = lax.all_to_all(pieces, "dp", 0, 0, tiled=True).sum(0, keepdims=True)
    spread = jnp.broadcast_to(mine, pieces.shape)
    return lax.all_to_all(spread, "dp", 0, 0, tiled=True).reshape(x.shape)


def make_shards(mesh):
    n = mesh.shape["dp"]
    half = n // 2
    shifts = tuple(range(1, half + 1)) + tuple((-s for s in range(1, n - half)))
    rings = tuple(((s, z_ring_pairs(mesh, s)) for s in shifts))
    dp_shifts = tuple(range(1, n))

    def shards(tokens, w_gate, w_up, w_down):
        c = lax.axis_index("expert") % 2
        width = tokens.shape[1] // 2
        part = lax.dynamic_slice_in_dim(tokens, c * width, width, axis=1)
        mine = gather_blocks(part, rings, n).reshape((-1, width))
        other = lax.ppermute(mine, "expert", [(i, i ^ 1) for i in range(mesh.shape["expert"])])
        low = jnp.where(c == 0, mine, other)
        high = jnp.where(c == 0, other, mine)
        block_rows = jnp.concatenate([low, high], axis=1)
        down_cols = transpose_blocks(w_down, n)
        gate = jnp.einsum("td,ehd->eth", block_rows, w_gate, preferred_element_type=jnp.float32)
        upward = jnp.einsum("td,ehd->eth", block_rows, w_up, preferred_element_type=jnp.float32)
        hidden = (jax.nn.silu(gate) * upward).astype(jnp.bfloat16)
        hidden_all = doubling_gather(hidden, n)
        outputs = jnp.einsum(
            "keth,ekhf->etf",
            hidden_all,
            down_cols.reshape(w_down.shape[0], n, -1, down_cols.shape[2]),
            preferred_element_type=jnp.float32,
        )
        features = outputs.astype(jnp.bfloat16)
        regrouped = lax.all_to_all(features, "expert", 1, 0, tiled=True)
        partial_gram = jnp.einsum(
            "etf,gtf->teg", regrouped, regrouped, preferred_element_type=jnp.float32
        )
        gram = all_reduce_dp(partial_gram, n)
        eye = jnp.eye(gram.shape[1], dtype=jnp.bool_)
        diagonal = jnp.sum(jnp.where(eye[None], gram, 0.0), axis=2)
        inverse = lax.rsqrt(diagonal + 1e-06)
        return gram * inverse[:, :, None] * inverse[:, None, :]

    return shards


def solution(mesh):
    placed = (
        P("dp", None),
        P("expert", "dp", None),
        P("expert", "dp", None),
        P("expert", "dp", None),
    )
    return jax.shard_map(
        make_shards(mesh),
        mesh=mesh,
        in_specs=placed,
        out_specs=P("expert", None, None),
        check_vma=False,
    )
```

profile of v0, /device:TPU:32, one launch (start us, length us, event | category | flops | bytes accessed | tf_op | source)
XLA Modules:
  0.0 199.1 jit_solution(7834840285856769042)
XLA Ops:
  0.0 1.0 bitcast_dynamic-update-slice_fusion.15
  1.0 3.8 %collective-permute-start = (bf16[32,1024]{1,0:T(8,128)(2,1)S(1)}, bf16[32,1024]{1,0:T(8,128)(2,1)S(1)}, u32[]{:S(2)}, u32[]{:S(2)}) collective-permute-start(bf16[32,1024]{1,0:T(8,128)(2,1)S(1)} %get-tuple-element.12), channel_id=1, source_target_pairs={{0,1},{1,2},{2,3},{3,4},{4,5},{5,6},{6,7},{7,16},{8,9},{9,10},{10,... | collective-permute-start | bytes 196616 | tf_op jit(solution)/shard_map/ppermute | solution.py:27
  4.8 6.4 %collective-permute-start.1 = (bf16[32,1024]{1,0:T(8,128)(2,1)S(1)}, bf16[32,1024]{1,0:T(8,128)(2,1)S(1)}, u32[]{:S(2)}, u32[]{:S(2)}) collective-permute-start(bf16[32,1024]{1,0:T(8,128)(2,1)S(1)} %get-tuple-element.12), channel_id=1, source_target_pairs={{0,2},{1,3},{2,4},{3,5},{4,6},{5,7},{6,16},{7,17},{8,10},{9,11},{1... | collective-permute-start | bytes 196616 | tf_op jit(solution)/shard_map/ppermute | solution.py:27
  11.2 6.5 %collective-permute-start.2 = (bf16[32,1024]{1,0:T(8,128)(2,1)S(1)}, bf16[32,1024]{1,0:T(8,128)(2,1)S(1)}, u32[]{:S(2)}, u32[]{:S(2)}) collective-permute-start(bf16[32,1024]{1,0:T(8,128)(2,1)S(1)} %get-tuple-element.12), channel_id=1, source_target_pairs={{0,3},{1,4},{2,5},{3,6},{4,7},{5,16},{6,17},{7,18},{8,11},{9,12},{... | collective-permute-start | bytes 196616 | tf_op jit(solution)/shard_map/ppermute | solution.py:27
  17.8 6.4 %collective-permute-start.3 = (bf16[32,1024]{1,0:T(8,128)(2,1)S(1)}, bf16[32,1024]{1,0:T(8,128)(2,1)S(1)}, u32[]{:S(2)}, u32[]{:S(2)}) collective-permute-start(bf16[32,1024]{1,0:T(8,128)(2,1)S(1)} %get-tuple-element.12), channel_id=1, source_target_pairs={{0,4},{1,5},{2,6},{3,7},{4,16},{5,17},{6,18},{7,19},{8,12},{9,13},... | collective-permute-start | bytes 196616 | tf_op jit(solution)/shard_map/ppermute | solution.py:27
  24.2 2.9 %collective-permute-start.4 = (bf16[32,1024]{1,0:T(8,128)(2,1)S(1)}, bf16[32,1024]{1,0:T(8,128)(2,1)S(1)}, u32[]{:S(2)}, u32[]{:S(2)}) collective-permute-start(bf16[32,1024]{1,0:T(8,128)(2,1)S(1)} %get-tuple-element.12), channel_id=1, source_target_pairs={{0,23},{1,0},{2,1},{3,2},{4,3},{5,4},{6,5},{7,6},{8,31},{9,8},{10,... | collective-permute-start | bytes 196616 | tf_op jit(solution)/shard_map/ppermute | solution.py:27
  27.9 1.0 sort.49
  28.9 1.0 sort.50
  30.8 0.8 constant_dynamic-slice_fusion
  31.7 4.6 %collective-permute-start.5 = (bf16[32,1024]{1,0:T(8,128)(2,1)S(1)}, bf16[32,1024]{1,0:T(8,128)(2,1)S(1)}, u32[]{:S(2)}, u32[]{:S(2)}) collective-permute-start(bf16[32,1024]{1,0:T(8,128)(2,1)S(1)} %get-tuple-element.12), channel_id=1, source_target_pairs={{0,22},{1,23},{2,0},{3,1},{4,2},{5,3},{6,4},{7,5},{8,30},{9,31},{1... | collective-permute-start | bytes 196616 | tf_op jit(solution)/shard_map/ppermute | solution.py:27
  36.3 1.9 collective-permute-start.6
  38.2 3.4 %collective-permute-start.11 = (bf16[2,96,256]{2,1,0:T(8,128)(2,1)}, bf16[2,96,256]{2,1,0:T(8,128)(2,1)S(1)}, u32[]{:S(2)}, u32[]{:S(2)}) collective-permute-start(bf16[2,96,256]{2,1,0:T(8,128)(2,1)} %get-tuple-element.20), channel_id=1, source_target_pairs={{0,1},{1,2},{2,3},{3,4},{4,5},{5,6},{6,7},{7,0},{8,9},{9,10},{10,1... | collective-permute-start | bytes 294920 | tf_op jit(solution)/shard_map/ppermute | solution.py:55
  41.6 6.0 %collective-permute-start.12 = (bf16[2,96,256]{2,1,0:T(8,128)(2,1)}, bf16[2,96,256]{2,1,0:T(8,128)(2,1)S(1)}, u32[]{:S(2)}, u32[]{:S(2)}) collective-permute-start(bf16[2,96,256]{2,1,0:T(8,128)(2,1)} %get-tuple-element.19), channel_id=1, source_target_pairs={{0,2},{1,3},{2,4},{3,5},{4,6},{5,7},{6,0},{7,1},{8,10},{9,11},{10,... | collective-permute-start | bytes 294920 | tf_op jit(solution)/shard_map/ppermute | solution.py:55
  47.7 2.6 %collective-permute-start.13 = (bf16[2,96,256]{2,1,0:T(8,128)(2,1)}, bf16[2,96,256]{2,1,0:T(8,128)(2,1)S(1)}, u32[]{:S(2)}, u32[]{:S(2)}) collective-permute-start(bf16[2,96,256]{2,1,0:T(8,128)(2,1)} %get-tuple-element.18), channel_id=1, source_target_pairs={{0,3},{1,4},{2,5},{3,6},{4,7},{5,0},{6,1},{7,2},{8,11},{9,12},{10,... | collective-permute-start | bytes 294920 | tf_op jit(solution)/shard_map/ppermute | solution.py:55
  50.3 5.4 %collective-permute-start.14 = (bf16[2,96,256]{2,1,0:T(8,128)(2,1)}, bf16[2,96,256]{2,1,0:T(8,128)(2,1)S(1)}, u32[]{:S(2)}, u32[]{:S(2)}) collective-permute-start(bf16[2,96,256]{2,1,0:T(8,128)(2,1)} %get-tuple-element.17), channel_id=1, source_target_pairs={{0,4},{1,5},{2,6},{3,7},{4,0},{5,1},{6,2},{7,3},{8,12},{9,13},{10,... | collective-permute-start | bytes 294920 | tf_op jit(solution)/shard_map/ppermute | solution.py:55
  55.7 5.8 %collective-permute-start.15 = (bf16[2,96,256]{2,1,0:T(8,128)(2,1)}, bf16[2,96,256]{2,1,0:T(8,128)(2,1)S(1)}, u32[]{:S(2)}, u32[]{:S(2)}) collective-permute-start(bf16[2,96,256]{2,1,0:T(8,128)(2,1)} %get-tuple-element.16), channel_id=1, source_target_pairs={{0,5},{1,6},{2,7},{3,0},{4,1},{5,2},{6,3},{7,4},{8,13},{9,14},{10,... | collective-permute-start | bytes 294920 | tf_op jit(solution)/shard_map/ppermute | solution.py:55
  62.3 1.9 collective-permute-start.7
  64.3 3.5 %collective-permute-start.16 = (bf16[2,96,256]{2,1,0:T(8,128)(2,1)S(1)}, bf16[2,96,256]{2,1,0:T(8,128)(2,1)S(1)}, u32[]{:S(2)}, u32[]{:S(2)}) collective-permute-start(bf16[2,96,256]{2,1,0:T(8,128)(2,1)S(1)} %copy-done.3), channel_id=1, source_target_pairs={{0,6},{1,7},{2,0},{3,1},{4,2},{5,3},{6,4},{7,5},{8,14},{9,15},{10,... | collective-permute-start | bytes 294920 | tf_op jit(solution)/shard_map/ppermute | solution.py:55
  67.8 6.0 %collective-permute-start.17 = (bf16[2,96,256]{2,1,0:T(8,128)(2,1)S(1)}, bf16[2,96,256]{2,1,0:T(8,128)(2,1)S(1)}, u32[]{:S(2)}, u32[]{:S(2)}) collective-permute-start(bf16[2,96,256]{2,1,0:T(8,128)(2,1)S(1)} %get-tuple-element.15), channel_id=1, source_target_pairs={{0,7},{1,0},{2,1},{3,2},{4,3},{5,4},{6,5},{7,6},{8,15},{9,8},{10,9... | collective-permute-start | bytes 294920 | tf_op jit(solution)/shard_map/ppermute | solution.py:55
  75.7 2.4 %collective-permute-start.8 = (bf16[1,2,256,96]{2,3,1,0:T(8,128)(2,1)S(1)}, bf16[1,2,256,96]{2,3,1,0:T(8,128)(2,1)S(1)}, u32[]{:S(2)}, u32[]{:S(2)}) collective-permute-start(bf16[1,2,256,96]{2,3,1,0:T(8,128)(2,1)S(1)} %fusion.3), channel_id=1, source_target_pairs={{0,4},{1,5},{2,6},{3,7},{4,0},{5,1},{6,2},{7,3},{8,12},{9,13},{10,... | collective-permute-start | bytes 294920 | tf_op jit(solution)/shard_map/ppermute | solution.py:41
  78.2 9.2 %collective-permute-done.8 = bf16[1,2,256,96]{2,3,1,0:T(8,128)(2,1)S(1)} collective-permute-done((bf16[1,2,256,96]{2,3,1,0:T(8,128)(2,1)S(1)}, bf16[1,2,256,96]{2,3,1,0:T(8,128)(2,1)S(1)}, u32[]{:S(2)}, u32[]{:S(2)}) %collective-permute-start.8) | collective-permute-done | bytes 98336 | tf_op jit(solution)/shard_map/ppermute | solution.py:41
  87.4 3.0 %collective-permute-start.9 = (bf16[2,2,256,96]{2,3,1,0:T(8,128)(2,1)S(1)}, bf16[2,2,256,96]{2,3,1,0:T(8,128)(2,1)S(1)}, u32[]{:S(2)}, u32[]{:S(2)}) collective-permute-start(bf16[2,2,256,96]{2,3,1,0:T(8,128)(2,1)S(1)} %pad_maximum_fusion.2), channel_id=1, source_target_pairs={{0,2},{1,3},{2,0},{3,1},{4,6},{5,7},{6,4},{7,5},{8,10},{9,11},{10,... | collective-permute-start | bytes 589832 | tf_op jit(solution)/shard_map/ppermute | solution.py:41
  90.5 8.6 %collective-permute-done.9 = bf16[2,2,256,96]{2,3,1,0:T(8,128)(2,1)S(1)} collective-permute-done((bf16[2,2,256,96]{2,3,1,0:T(8,128)(2,1)S(1)}, bf16[2,2,256,96]{2,3,1,0:T(8,128)(2,1)S(1)}, u32[]{:S(2)}, u32[]{:S(2)}) %collective-permute-start.9) | collective-permute-done | bytes 196640 | tf_op jit(solution)/shard_map/ppermute | solution.py:41
  99.1 5.5 %collective-permute-start.10 = (bf16[4,2,256,96]{2,3,1,0:T(8,128)(2,1)S(1)}, bf16[4,2,256,96]{2,3,1,0:T(8,128)(2,1)}, u32[]{:S(2)}, u32[]{:S(2)}) collective-permute-start(bf16[4,2,256,96]{2,3,1,0:T(8,128)(2,1)S(1)} %pad_maximum_fusion.1), channel_id=1, source_target_pairs={{0,1},{1,0},{2,3},{3,2},{4,5},{5,4},{6,7},{7,6},{8,9},{9,8},{10,11... | collective-permute-start | bytes 1179656 | tf_op jit(solution)/shard_map/ppermute | solution.py:41
  105.3 8.7 %collective-permute-done.10 = bf16[4,2,256,96]{2,3,1,0:T(8,128)(2,1)} collective-permute-done((bf16[4,2,256,96]{2,3,1,0:T(8,128)(2,1)S(1)}, bf16[4,2,256,96]{2,3,1,0:T(8,128)(2,1)}, u32[]{:S(2)}, u32[]{:S(2)}) %collective-permute-start.10) | collective-permute-done | bytes 393248 | tf_op jit(solution)/shard_map/ppermute | solution.py:41
  114.0 1.1 pad_maximum_fusion
  116.5 39.1 %all_to_all.33 = bf16[2,256,256]{2,0,1:T(2,128)(2,1)S(1)} all-to-all(bf16[2,256,256]{2,0,1:T(2,128)(2,1)S(1)} %copy.13), channel_id=1, replica_groups=mesh['expert'=64,'dp'=8] {'expert'}, dimensions={1} | all-to-all | bytes 524288 | tf_op jit(solution)/shard_map/all_to_all | solution.py:97
  156.1 19.5 %all_to_all.34 = f32[8,1,8192]{2,1,0:T(1,128)S(1)} all-to-all(f32[8,1,8192]{2,1,0:T(1,128)S(1)} %bitcast.87), channel_id=1, replica_groups=mesh['expert'=64,'dp'=8] {'dp'}, dimensions={0} | all-to-all | bytes 524288 | tf_op jit(solution)/shard_map/all_to_all | solution.py:64
  175.9 0.8 broadcast_in_dim.74
  176.7 5.5 %all-to-all-start.2 = ((f32[8,1,8192]{2,1,0:T(1,128)}), f32[8,1,8192]{2,1,0:T(1,128)S(1)}, u32[]{:S(2)}, u32[]{:S(2)}) async-start(f32[8,1,8192]{2,1,0:T(1,128)} %broadcast_in_dim.74), calls=%async_computation.2 | async-start | bytes 524288 | tf_op jit(solution)/shard_map/all_to_all | solution.py:66
  182.2 15.9 %all-to-all-done.2 = f32[8,1,8192]{2,1,0:T(1,128)S(1)} async-done(((f32[8,1,8192]{2,1,0:T(1,128)}), f32[8,1,8192]{2,1,0:T(1,128)S(1)}, u32[]{:S(2)}, u32[]{:S(2)}) %all-to-all-start.2) | async-done | bytes 262176 | tf_op jit(solution)/shard_map/all_to_all | solution.py:66
  198.3 0.9 fusion.12
  (75 shorter events, 7.1 us)
Async XLA Ops:
  0.0 74.0 %copy-start = (bf16[2,96,2048]{2,1,0:T(8,128)(2,1)S(1)}, bf16[2,96,2048]{2,1,0:T(8,128)(2,1)}, u32[]{:S(2)}) copy-start(bf16[2,96,2048]{2,1,0:T(8,128)(2,1)} %param.7) | copy-start | bytes 2359300
  0.0 29.9 %copy-start.1 = (s32[8]{0:T(128)S(1)}, s32[8]{0:T(128)}, u32[]{:S(2)}) copy-start(s32[8]{0:T(128)} %constant.142) | copy-start | bytes 100
  0.0 30.7 %copy-start.2 = (bf16[2,96,2048]{2,1,0:T(8,128)(2,1)S(1)}, bf16[2,96,2048]{2,1,0:T(8,128)(2,1)}, u32[]{:S(2)}) copy-start(bf16[2,96,2048]{2,1,0:T(8,128)(2,1)} %param.9) | copy-start | bytes 2359300
  1.0 30.6 %collective-permute-start = (bf16[32,1024]{1,0:T(8,128)(2,1)S(1)}, bf16[32,1024]{1,0:T(8,128)(2,1)S(1)}, u32[]{:S(2)}, u32[]{:S(2)}) collective-permute-start(bf16[32,1024]{1,0:T(8,128)(2,1)S(1)} %get-tuple-element.12), channel_id=1, source_target_pairs={{0,1},{1,2},{2,3},{3,4},{4,5},{5,6},{6,7},{7,16},{8,9},{9,10},{10,... | collective-permute-start | bytes 196616 | tf_op jit(solution)/shard_map/ppermute | solution.py:27
  4.8 31.4 %collective-permute-start.1 = (bf16[32,1024]{1,0:T(8,128)(2,1)S(1)}, bf16[32,1024]{1,0:T(8,128)(2,1)S(1)}, u32[]{:S(2)}, u32[]{:S(2)}) collective-permute-start(bf16[32,1024]{1,0:T(8,128)(2,1)S(1)} %get-tuple-element.12), channel_id=1, source_target_pairs={{0,2},{1,3},{2,4},{3,5},{4,6},{5,7},{6,16},{7,17},{8,10},{9,11},{1... | collective-permute-start | bytes 196616 | tf_op jit(solution)/shard_map/ppermute | solution.py:27
  11.2 27.0 %collective-permute-start.2 = (bf16[32,1024]{1,0:T(8,128)(2,1)S(1)}, bf16[32,1024]{1,0:T(8,128)(2,1)S(1)}, u32[]{:S(2)}, u32[]{:S(2)}) collective-permute-start(bf16[32,1024]{1,0:T(8,128)(2,1)S(1)} %get-tuple-element.12), channel_id=1, source_target_pairs={{0,3},{1,4},{2,5},{3,6},{4,7},{5,16},{6,17},{7,18},{8,11},{9,12},{... | collective-permute-start | bytes 196616 | tf_op jit(solution)/shard_map/ppermute | solution.py:27
  17.8 23.8 %collective-permute-start.3 = (bf16[32,1024]{1,0:T(8,128)(2,1)S(1)}, bf16[32,1024]{1,0:T(8,128)(2,1)S(1)}, u32[]{:S(2)}, u32[]{:S(2)}) collective-permute-start(bf16[32,1024]{1,0:T(8,128)(2,1)S(1)} %get-tuple-element.12), channel_id=1, source_target_pairs={{0,4},{1,5},{2,6},{3,7},{4,16},{5,17},{6,18},{7,19},{8,12},{9,13},... | collective-permute-start | bytes 196616 | tf_op jit(solution)/shard_map/ppermute | solution.py:27
  24.2 23.5 %collective-permute-start.4 = (bf16[32,1024]{1,0:T(8,128)(2,1)S(1)}, bf16[32,1024]{1,0:T(8,128)(2,1)S(1)}, u32[]{:S(2)}, u32[]{:S(2)}) collective-permute-start(bf16[32,1024]{1,0:T(8,128)(2,1)S(1)} %get-tuple-element.12), channel_id=1, source_target_pairs={{0,23},{1,0},{2,1},{3,2},{4,3},{5,4},{6,5},{7,6},{8,31},{9,8},{10,... | collective-permute-start | bytes 196616 | tf_op jit(solution)/shard_map/ppermute | solution.py:27
  31.7 18.7 %collective-permute-start.5 = (bf16[32,1024]{1,0:T(8,128)(2,1)S(1)}, bf16[32,1024]{1,0:T(8,128)(2,1)S(1)}, u32[]{:S(2)}, u32[]{:S(2)}) collective-permute-start(bf16[32,1024]{1,0:T(8,128)(2,1)S(1)} %get-tuple-element.12), channel_id=1, source_target_pairs={{0,22},{1,23},{2,0},{3,1},{4,2},{5,3},{6,4},{7,5},{8,30},{9,31},{1... | collective-permute-start | bytes 196616 | tf_op jit(solution)/shard_map/ppermute | solution.py:27
  36.3 19.5 %collective-permute-start.6 = (bf16[32,1024]{1,0:T(8,128)(2,1)S(1)}, bf16[32,1024]{1,0:T(8,128)(2,1)S(1)}, u32[]{:S(2)}, u32[]{:S(2)}) collective-permute-start(bf16[32,1024]{1,0:T(8,128)(2,1)S(1)} %get-tuple-element.12), channel_id=1, source_target_pairs={{0,21},{1,22},{2,23},{3,0},{4,1},{5,2},{6,3},{7,4},{8,29},{9,30},{... | collective-permute-start | bytes 196616 | tf_op jit(solution)/shard_map/ppermute | solution.py:27
  38.2 24.1 %collective-permute-start.11 = (bf16[2,96,256]{2,1,0:T(8,128)(2,1)}, bf16[2,96,256]{2,1,0:T(8,128)(2,1)S(1)}, u32[]{:S(2)}, u32[]{:S(2)}) collective-permute-start(bf16[2,96,256]{2,1,0:T(8,128)(2,1)} %get-tuple-element.20), channel_id=1, source_target_pairs={{0,1},{1,2},{2,3},{3,4},{4,5},{5,6},{6,7},{7,0},{8,9},{9,10},{10,1... | collective-permute-start | bytes 294920 | tf_op jit(solution)/shard_map/ppermute | solution.py:55
  41.6 22.7 %collective-permute-start.12 = (bf16[2,96,256]{2,1,0:T(8,128)(2,1)}, bf16[2,96,256]{2,1,0:T(8,128)(2,1)S(1)}, u32[]{:S(2)}, u32[]{:S(2)}) collective-permute-start(bf16[2,96,256]{2,1,0:T(8,128)(2,1)} %get-tuple-element.19), channel_id=1, source_target_pairs={{0,2},{1,3},{2,4},{3,5},{4,6},{5,7},{6,0},{7,1},{8,10},{9,11},{10,... | collective-permute-start | bytes 294920 | tf_op jit(solution)/shard_map/ppermute | solution.py:55
  47.7 20.1 %collective-permute-start.13 = (bf16[2,96,256]{2,1,0:T(8,128)(2,1)}, bf16[2,96,256]{2,1,0:T(8,128)(2,1)S(1)}, u32[]{:S(2)}, u32[]{:S(2)}) collective-permute-start(bf16[2,96,256]{2,1,0:T(8,128)(2,1)} %get-tuple-element.18), channel_id=1, source_target_pairs={{0,3},{1,4},{2,5},{3,6},{4,7},{5,0},{6,1},{7,2},{8,11},{9,12},{10,... | collective-permute-start | bytes 294920 | tf_op jit(solution)/shard_map/ppermute | solution.py:55
  50.3 27.8 %collective-permute-start.14 = (bf16[2,96,256]{2,1,0:T(8,128)(2,1)}, bf16[2,96,256]{2,1,0:T(8,128)(2,1)S(1)}, u32[]{:S(2)}, u32[]{:S(2)}) collective-permute-start(bf16[2,96,256]{2,1,0:T(8,128)(2,1)} %get-tuple-element.17), channel_id=1, source_target_pairs={{0,4},{1,5},{2,6},{3,7},{4,0},{5,1},{6,2},{7,3},{8,12},{9,13},{10,... | collective-permute-start | bytes 294920 | tf_op jit(solution)/shard_map/ppermute | solution.py:55
  55.7 34.7 %collective-permute-start.15 = (bf16[2,96,256]{2,1,0:T(8,128)(2,1)}, bf16[2,96,256]{2,1,0:T(8,128)(2,1)S(1)}, u32[]{:S(2)}, u32[]{:S(2)}) collective-permute-start(bf16[2,96,256]{2,1,0:T(8,128)(2,1)} %get-tuple-element.16), channel_id=1, source_target_pairs={{0,5},{1,6},{2,7},{3,0},{4,1},{5,2},{6,3},{7,4},{8,13},{9,14},{10,... | collective-permute-start | bytes 294920 | tf_op jit(solution)/shard_map/ppermute | solution.py:55
  62.2 2.1 %copy-start.3 = (bf16[2,96,256]{2,1,0:T(8,128)(2,1)S(1)}, bf16[2,96,256]{2,1,0:T(8,128)(2,1)}, u32[]{:S(2)}) copy-start(bf16[2,96,256]{2,1,0:T(8,128)(2,1)} %get-tuple-element.21) | copy-start | bytes 294916
  62.3 11.5 %collective-permute-start.7 = (bf16[256,1024]{1,0:T(8,128)(2,1)S(1)}, bf16[256,1024]{1,0:T(8,128)(2,1)S(1)}, u32[]{:S(2)}, u32[]{:S(2)}) collective-permute-start(bf16[256,1024]{1,0:T(8,128)(2,1)S(1)} %bitcast_select_fusion), channel_id=1, source_target_pairs={{0,8},{8,0},{16,24},{24,16},{32,40},{40,32},{48,56},{56,48},{64,72... | collective-permute-start | bytes 1572872 | tf_op jit(solution)/shard_map/ppermute | solution.py:81
  64.3 40.4 %collective-permute-start.16 = (bf16[2,96,256]{2,1,0:T(8,128)(2,1)S(1)}, bf16[2,96,256]{2,1,0:T(8,128)(2,1)S(1)}, u32[]{:S(2)}, u32[]{:S(2)}) collective-permute-start(bf16[2,96,256]{2,1,0:T(8,128)(2,1)S(1)} %copy-done.3), channel_id=1, source_target_pairs={{0,6},{1,7},{2,0},{3,1},{4,2},{5,3},{6,4},{7,5},{8,14},{9,15},{10,... | collective-permute-start | bytes 294920 | tf_op jit(solution)/shard_map/ppermute | solution.py:55
  67.8 36.9 %collective-permute-start.17 = (bf16[2,96,256]{2,1,0:T(8,128)(2,1)S(1)}, bf16[2,96,256]{2,1,0:T(8,128)(2,1)S(1)}, u32[]{:S(2)}, u32[]{:S(2)}) collective-permute-start(bf16[2,96,256]{2,1,0:T(8,128)(2,1)S(1)} %get-tuple-element.15), channel_id=1, source_target_pairs={{0,7},{1,0},{2,1},{3,2},{4,3},{5,4},{6,5},{7,6},{8,15},{9,8},{10,9... | collective-permute-start | bytes 294920 | tf_op jit(solution)/shard_map/ppermute | solution.py:55
  74.1 1.1 copy-start.4
  75.7 11.7 %collective-permute-start.8 = (bf16[1,2,256,96]{2,3,1,0:T(8,128)(2,1)S(1)}, bf16[1,2,256,96]{2,3,1,0:T(8,128)(2,1)S(1)}, u32[]{:S(2)}, u32[]{:S(2)}) collective-permute-start(bf16[1,2,256,96]{2,3,1,0:T(8,128)(2,1)S(1)} %fusion.3), channel_id=1, source_target_pairs={{0,4},{1,5},{2,6},{3,7},{4,0},{5,1},{6,2},{7,3},{8,12},{9,13},{10,... | collective-permute-start | bytes 294920 | tf_op jit(solution)/shard_map/ppermute | solution.py:41
  87.4 11.6 %collective-permute-start.9 = (bf16[2,2,256,96]{2,3,1,0:T(8,128)(2,1)S(1)}, bf16[2,2,256,96]{2,3,1,0:T(8,128)(2,1)S(1)}, u32[]{:S(2)}, u32[]{:S(2)}) collective-permute-start(bf16[2,2,256,96]{2,3,1,0:T(8,128)(2,1)S(1)} %pad_maximum_fusion.2), channel_id=1, source_target_pairs={{0,2},{1,3},{2,0},{3,1},{4,6},{5,7},{6,4},{7,5},{8,10},{9,11},{10,... | collective-permute-start | bytes 589832 | tf_op jit(solution)/shard_map/ppermute | solution.py:41
  99.1 14.9 %collective-permute-start.10 = (bf16[4,2,256,96]{2,3,1,0:T(8,128)(2,1)S(1)}, bf16[4,2,256,96]{2,3,1,0:T(8,128)(2,1)}, u32[]{:S(2)}, u32[]{:S(2)}) collective-permute-start(bf16[4,2,256,96]{2,3,1,0:T(8,128)(2,1)S(1)} %pad_maximum_fusion.1), channel_id=1, source_target_pairs={{0,1},{1,0},{2,3},{3,2},{4,5},{5,4},{6,7},{7,6},{8,9},{9,8},{10,11... | collective-permute-start | bytes 1179656 | tf_op jit(solution)/shard_map/ppermute | solution.py:41
  176.7 21.4 %all-to-all-start.2 = ((f32[8,1,8192]{2,1,0:T(1,128)}), f32[8,1,8192]{2,1,0:T(1,128)S(1)}, u32[]{:S(2)}, u32[]{:S(2)}) async-start(f32[8,1,8192]{2,1,0:T(1,128)} %broadcast_in_dim.74), calls=%async_computation.2 | async-start | bytes 524288 | tf_op jit(solution)/shard_map/all_to_all | solution.py:66
where the time goes:
time: 200 us; the launch traced here: 199 us
  starting transfers between devices  83.7 us (42%)
  blocking collectives  58.6 us (29%)
  waiting for transfers between devices  42.5 us (21%)
  local copies, waits for them, and re-layouts  6.55 us (3%)
  other arithmetic  5.31 us (3%)
    all_to_all x1, blocking collectives, shards(): regrouped = lax.all_to_all(features, 'expert', 1, 0, tiled=True)  39.1 us
    ppermute x7, starting transfers between devices, transpose_blocks(): got.append(lax.ppermute(piece, 'dp', [(i, (i + s) % n) for i in range(n)]))  32.7 us
    ppermute x7, starting transfers between devices, gather_blocks(): lax.ppermute(block, BOTH, pairs)  32.6 us
    ppermute x3, waiting for transfers between devices, doubling_gather(): have = jnp.concatenate([have, lax.ppermute(have, 'dp', pairs)], axis=0)  26.6 us
    all_to_all x1, blocking collectives, all_reduce_dp(): mine = lax.all_to_all(pieces, 'dp', 0, 0, tiled=True).sum(0, keepdims=True)  19.5 us
    all_to_all x1, waiting for transfers between devices, all_reduce_dp(): return lax.all_to_all(spread, 'dp', 0, 0, tiled=True).reshape(x.shape)  15.9 us
    ppermute x3, starting transfers between devices, doubling_gather(): have = jnp.concatenate([have, lax.ppermute(have, 'dp', pairs)], axis=0)  11 us
    all_to_all x1, starting transfers between devices, all_reduce_dp(): return lax.all_to_all(spread, 'dp', 0, 0, tiled=True).reshape(x.shape)  5.52 us
  transfers between devices with their start and end apart: 19, of which 4 were waited for; matrix products, arithmetic and copies ran while one was open for 4% of the time, Pallas kernels for 0%

commit v1 on v0

--- a/solution.py
+++ b/solution.py
@@ -94,7 +94,10 @@
             preferred_element_type=jnp.float32,
         )
         features = outputs.astype(jnp.bfloat16)
-        regrouped = lax.all_to_all(features, "expert", 1, 0, tiled=True)
+        carry_in = lax.all_to_all(
+            jnp.stack(jnp.split(features, lax.axis_size("expert"), axis=1)), "expert", 0, 0
+        )
+        regrouped = jnp.concatenate(carry_in, axis=0)
         partial_gram = jnp.einsum(
             "etf,gtf->teg", regrouped, regrouped, preferred_element_type=jnp.float32
         )

time: 200 us -> 200 us (level)
  no operation moved by 1% of the time
where the time goes in v1:
time: 200 us
  starting transfers between devices  83.7 us (42%)
  blocking collectives  58.6 us (29%)
  waiting for transfers between devices  42.5 us (21%)
  local copies, waits for them, and re-layouts  6.78 us (3%)
  other arithmetic  5.31 us (3%)
    all_to_all x1, blocking collectives, shards(): lax.all_to_all(jnp.stack(jnp.split(features, lax.axis_size('expert'), axi...  39.1 us
    ppermute x7, starting transfers between devices, transpose_blocks(): got.append(lax.ppermute(piece, 'dp', [(i, (i + s) % n) for i in range(n)]))  32.7 us
    ppermute x7, starting transfers between devices, gather_blocks(): lax.ppermute(block, BOTH, pairs)  32.6 us
    ppermute x3, waiting for transfers between devices, doubling_gather(): have = jnp.concatenate([have, lax.ppermute(have, 'dp', pairs)], axis=0)  26.6 us
    all_to_all x1, blocking collectives, all_reduce_dp(): mine = lax.all_to_all(pieces, 'dp', 0, 0, tiled=True).sum(0, keepdims=True)  19.5 us
    all_to_all x1, waiting for transfers between devices, all_reduce_dp(): return lax.all_to_all(spread, 'dp', 0, 0, tiled=True).reshape(x.shape)  15.9 us
    ppermute x3, starting transfers between devices, doubling_gather(): have = jnp.concatenate([have, lax.ppermute(have, 'dp', pairs)], axis=0)  11 us
    all_to_all x1, starting transfers between devices, all_reduce_dp(): return lax.all_to_all(spread, 'dp', 0, 0, tiled=True).reshape(x.shape)  5.52 us
  transfers between devices with their start and end apart: 19, of which 4 were waited for; matrix products, arithmetic and copies ran while one was open for 4% of the time, Pallas kernels for 0%

profile of v1, /device:TPU:32, one launch (start us, length us, event | category | flops | bytes accessed | tf_op | source)
XLA Modules:
  0.0 199.6 jit_solution(12331619717950925229)
XLA Ops:
  0.0 1.0 constant_dynamic-update-slice_fusion.7
  1.0 3.8 %collective-permute-start = (bf16[32,1024]{1,0:T(8,128)(2,1)S(1)}, bf16[32,1024]{1,0:T(8,128)(2,1)S(1)}, u32[]{:S(2)}, u32[]{:S(2)}) collective-permute-start(bf16[32,1024]{1,0:T(8,128)(2,1)S(1)} %get-tuple-element.12), channel_id=1, source_target_pairs={{0,1},{1,2},{2,3},{3,4},{4,5},{5,6},{6,7},{7,16},{8,9},{9,10},{10,... | collective-permute-start | bytes 196616 | tf_op jit(solution)/shard_map/ppermute | solution.py:27
  4.8 6.4 %collective-permute-start.1 = (bf16[32,1024]{1,0:T(8,128)(2,1)S(1)}, bf16[32,1024]{1,0:T(8,128)(2,1)S(1)}, u32[]{:S(2)}, u32[]{:S(2)}) collective-permute-start(bf16[32,1024]{1,0:T(8,128)(2,1)S(1)} %get-tuple-element.12), channel_id=1, source_target_pairs={{0,2},{1,3},{2,4},{3,5},{4,6},{5,7},{6,16},{7,17},{8,10},{9,11},{1... | collective-permute-start | bytes 196616 | tf_op jit(solution)/shard_map/ppermute | solution.py:27
  11.2 6.5 %collective-permute-start.2 = (bf16[32,1024]{1,0:T(8,128)(2,1)S(1)}, bf16[32,1024]{1,0:T(8,128)(2,1)S(1)}, u32[]{:S(2)}, u32[]{:S(2)}) collective-permute-start(bf16[32,1024]{1,0:T(8,128)(2,1)S(1)} %get-tuple-element.12), channel_id=1, source_target_pairs={{0,3},{1,4},{2,5},{3,6},{4,7},{5,16},{6,17},{7,18},{8,11},{9,12},{... | collective-permute-start | bytes 196616 | tf_op jit(solution)/shard_map/ppermute | solution.py:27
  17.8 6.4 %collective-permute-start.3 = (bf16[32,1024]{1,0:T(8,128)(2,1)S(1)}, bf16[32,1024]{1,0:T(8,128)(2,1)S(1)}, u32[]{:S(2)}, u32[]{:S(2)}) collective-permute-start(bf16[32,1024]{1,0:T(8,128)(2,1)S(1)} %get-tuple-element.12), channel_id=1, source_target_pairs={{0,4},{1,5},{2,6},{3,7},{4,16},{5,17},{6,18},{7,19},{8,12},{9,13},... | collective-permute-start | bytes 196616 | tf_op jit(solution)/shard_map/ppermute | solution.py:27
  24.2 2.9 %collective-permute-start.4 = (bf16[32,1024]{1,0:T(8,128)(2,1)S(1)}, bf16[32,1024]{1,0:T(8,128)(2,1)S(1)}, u32[]{:S(2)}, u32[]{:S(2)}) collective-permute-start(bf16[32,1024]{1,0:T(8,128)(2,1)S(1)} %get-tuple-element.12), channel_id=1, source_target_pairs={{0,23},{1,0},{2,1},{3,2},{4,3},{5,4},{6,5},{7,6},{8,31},{9,8},{10,... | collective-permute-start | bytes 196616 | tf_op jit(solution)/shard_map/ppermute | solution.py:27
  27.9 1.0 sort.49
  28.9 1.0 sort.50
  30.8 0.8 constant_dynamic-slice_fusion
  31.7 4.6 %collective-permute-start.5 = (bf16[32,1024]{1,0:T(8,128)(2,1)S(1)}, bf16[32,1024]{1,0:T(8,128)(2,1)S(1)}, u32[]{:S(2)}, u32[]{:S(2)}) collective-permute-start(bf16[32,1024]{1,0:T(8,128)(2,1)S(1)} %get-tuple-element.12), channel_id=1, source_target_pairs={{0,22},{1,23},{2,0},{3,1},{4,2},{5,3},{6,4},{7,5},{8,30},{9,31},{1... | collective-permute-start | bytes 196616 | tf_op jit(solution)/shard_map/ppermute | solution.py:27
  36.3 1.9 collective-permute-start.6
  38.2 3.4 %collective-permute-start.11 = (bf16[2,96,256]{2,1,0:T(8,128)(2,1)}, bf16[2,96,256]{2,1,0:T(8,128)(2,1)S(1)}, u32[]{:S(2)}, u32[]{:S(2)}) collective-permute-start(bf16[2,96,256]{2,1,0:T(8,128)(2,1)} %get-tuple-element.20), channel_id=1, source_target_pairs={{0,1},{1,2},{2,3},{3,4},{4,5},{5,6},{6,7},{7,0},{8,9},{9,10},{10,1... | collective-permute-start | bytes 294920 | tf_op jit(solution)/shard_map/ppermute | solution.py:55
  41.6 6.0 %collective-permute-start.12 = (bf16[2,96,256]{2,1,0:T(8,128)(2,1)}, bf16[2,96,256]{2,1,0:T(8,128)(2,1)S(1)}, u32[]{:S(2)}, u32[]{:S(2)}) collective-permute-start(bf16[2,96,256]{2,1,0:T(8,128)(2,1)} %get-tuple-element.19), channel_id=1, source_target_pairs={{0,2},{1,3},{2,4},{3,5},{4,6},{5,7},{6,0},{7,1},{8,10},{9,11},{10,... | collective-permute-start | bytes 294920 | tf_op jit(solution)/shard_map/ppermute | solution.py:55
  47.7 2.6 %collective-permute-start.13 = (bf16[2,96,256]{2,1,0:T(8,128)(2,1)}, bf16[2,96,256]{2,1,0:T(8,128)(2,1)S(1)}, u32[]{:S(2)}, u32[]{:S(2)}) collective-permute-start(bf16[2,96,256]{2,1,0:T(8,128)(2,1)} %get-tuple-element.18), channel_id=1, source_target_pairs={{0,3},{1,4},{2,5},{3,6},{4,7},{5,0},{6,1},{7,2},{8,11},{9,12},{10,... | collective-permute-start | bytes 294920 | tf_op jit(solution)/shard_map/ppermute | solution.py:55
  50.3 5.4 %collective-permute-start.14 = (bf16[2,96,256]{2,1,0:T(8,128)(2,1)}, bf16[2,96,256]{2,1,0:T(8,128)(2,1)S(1)}, u32[]{:S(2)}, u32[]{:S(2)}) collective-permute-start(bf16[2,96,256]{2,1,0:T(8,128)(2,1)} %get-tuple-element.17), channel_id=1, source_target_pairs={{0,4},{1,5},{2,6},{3,7},{4,0},{5,1},{6,2},{7,3},{8,12},{9,13},{10,... | collective-permute-start | bytes 294920 | tf_op jit(solution)/shard_map/ppermute | solution.py:55
  55.7 5.8 %collective-permute-start.15 = (bf16[2,96,256]{2,1,0:T(8,128)(2,1)}, bf16[2,96,256]{2,1,0:T(8,128)(2,1)S(1)}, u32[]{:S(2)}, u32[]{:S(2)}) collective-permute-start(bf16[2,96,256]{2,1,0:T(8,128)(2,1)} %get-tuple-element.16), channel_id=1, source_target_pairs={{0,5},{1,6},{2,7},{3,0},{4,1},{5,2},{6,3},{7,4},{8,13},{9,14},{10,... | collective-permute-start | bytes 294920 | tf_op jit(solution)/shard_map/ppermute | solution.py:55
  62.3 1.9 collective-permute-start.7
  64.3 3.5 %collective-permute-start.16 = (bf16[2,96,256]{2,1,0:T(8,128)(2,1)S(1)}, bf16[2,96,256]{2,1,0:T(8,128)(2,1)S(1)}, u32[]{:S(2)}, u32[]{:S(2)}) collective-permute-start(bf16[2,96,256]{2,1,0:T(8,128)(2,1)S(1)} %copy-done.3), channel_id=1, source_target_pairs={{0,6},{1,7},{2,0},{3,1},{4,2},{5,3},{6,4},{7,5},{8,14},{9,15},{10,... | collective-permute-start | bytes 294920 | tf_op jit(solution)/shard_map/ppermute | solution.py:55
  67.8 6.0 %collective-permute-start.17 = (bf16[2,96,256]{2,1,0:T(8,128)(2,1)S(1)}, bf16[2,96,256]{2,1,0:T(8,128)(2,1)S(1)}, u32[]{:S(2)}, u32[]{:S(2)}) collective-permute-start(bf16[2,96,256]{2,1,0:T(8,128)(2,1)S(1)} %get-tuple-element.15), channel_id=1, source_target_pairs={{0,7},{1,0},{2,1},{3,2},{4,3},{5,4},{6,5},{7,6},{8,15},{9,8},{10,9... | collective-permute-start | bytes 294920 | tf_op jit(solution)/shard_map/ppermute | solution.py:55
  75.7 2.4 %collective-permute-start.8 = (bf16[1,2,256,96]{2,3,1,0:T(8,128)(2,1)S(1)}, bf16[1,2,256,96]{2,3,1,0:T(8,128)(2,1)S(1)}, u32[]{:S(2)}, u32[]{:S(2)}) collective-permute-start(bf16[1,2,256,96]{2,3,1,0:T(8,128)(2,1)S(1)} %fusion.3), channel_id=1, source_target_pairs={{0,4},{1,5},{2,6},{3,7},{4,0},{5,1},{6,2},{7,3},{8,12},{9,13},{10,... | collective-permute-start | bytes 294920 | tf_op jit(solution)/shard_map/ppermute | solution.py:41
  78.2 9.2 %collective-permute-done.8 = bf16[1,2,256,96]{2,3,1,0:T(8,128)(2,1)S(1)} collective-permute-done((bf16[1,2,256,96]{2,3,1,0:T(8,128)(2,1)S(1)}, bf16[1,2,256,96]{2,3,1,0:T(8,128)(2,1)S(1)}, u32[]{:S(2)}, u32[]{:S(2)}) %collective-permute-start.8) | collective-permute-done | bytes 98336 | tf_op jit(solution)/shard_map/ppermute | solution.py:41
  87.4 3.0 %collective-permute-start.9 = (bf16[2,2,256,96]{2,3,1,0:T(8,128)(2,1)S(1)}, bf16[2,2,256,96]{2,3,1,0:T(8,128)(2,1)S(1)}, u32[]{:S(2)}, u32[]{:S(2)}) collective-permute-start(bf16[2,2,256,96]{2,3,1,0:T(8,128)(2,1)S(1)} %pad_maximum_fusion.2), channel_id=1, source_target_pairs={{0,2},{1,3},{2,0},{3,1},{4,6},{5,7},{6,4},{7,5},{8,10},{9,11},{10,... | collective-permute-start | bytes 589832 | tf_op jit(solution)/shard_map/ppermute | solution.py:41
  90.5 8.6 %collective-permute-done.9 = bf16[2,2,256,96]{2,3,1,0:T(8,128)(2,1)S(1)} collective-permute-done((bf16[2,2,256,96]{2,3,1,0:T(8,128)(2,1)S(1)}, bf16[2,2,256,96]{2,3,1,0:T(8,128)(2,1)S(1)}, u32[]{:S(2)}, u32[]{:S(2)}) %collective-permute-start.9) | collective-permute-done | bytes 196640 | tf_op jit(solution)/shard_map/ppermute | solution.py:41
  99.1 5.5 %collective-permute-start.10 = (bf16[4,2,256,96]{2,3,1,0:T(8,128)(2,1)S(1)}, bf16[4,2,256,96]{2,3,1,0:T(8,128)(2,1)}, u32[]{:S(2)}, u32[]{:S(2)}) collective-permute-start(bf16[4,2,256,96]{2,3,1,0:T(8,128)(2,1)S(1)} %pad_maximum_fusion.1), channel_id=1, source_target_pairs={{0,1},{1,0},{2,3},{3,2},{4,5},{5,4},{6,7},{7,6},{8,9},{9,8},{10,11... | collective-permute-start | bytes 1179656 | tf_op jit(solution)/shard_map/ppermute | solution.py:41
  105.3 8.7 %collective-permute-done.10 = bf16[4,2,256,96]{2,3,1,0:T(8,128)(2,1)} collective-permute-done((bf16[4,2,256,96]{2,3,1,0:T(8,128)(2,1)S(1)}, bf16[4,2,256,96]{2,3,1,0:T(8,128)(2,1)}, u32[]{:S(2)}, u32[]{:S(2)}) %collective-permute-start.10) | collective-permute-done | bytes 393248 | tf_op jit(solution)/shard_map/ppermute | solution.py:41
  114.0 1.1 pad_maximum_fusion
  117.2 39.1 %all_to_all.20 = bf16[64,2,4,256]{3,2,1,0:T(4,128)(2,1)S(1)} all-to-all(bf16[64,2,4,256]{3,2,1,0:T(4,128)(2,1)S(1)} %constant_dynamic-update-slice_fusion.16), channel_id=1, replica_groups=mesh['expert'=64,'dp'=8] {'expert'}, dimensions={0} | all-to-all | bytes 524288 | tf_op jit(solution)/shard_map/all_to_all | solution.py:97
  156.5 19.5 %all_to_all.21 = f32[8,1,8192]{2,1,0:T(1,128)S(1)} all-to-all(f32[8,1,8192]{2,1,0:T(1,128)S(1)} %bitcast.337), channel_id=1, replica_groups=mesh['expert'=64,'dp'=8] {'dp'}, dimensions={0} | all-to-all | bytes 524288 | tf_op jit(solution)/shard_map/all_to_all | solution.py:64
  176.3 0.8 broadcast_in_dim.74
  177.1 5.5 %all-to-all-start.2 = ((f32[8,1,8192]{2,1,0:T(1,128)}), f32[8,1,8192]{2,1,0:T(1,128)S(1)}, u32[]{:S(2)}, u32[]{:S(2)}) async-start(f32[8,1,8192]{2,1,0:T(1,128)} %broadcast_in_dim.74), calls=%async_computation.2 | async-start | bytes 524288 | tf_op jit(solution)/shard_map/all_to_all | solution.py:66
  182.7 15.9 %all-to-all-done.2 = f32[8,1,8192]{2,1,0:T(1,128)S(1)} async-done(((f32[8,1,8192]{2,1,0:T(1,128)}), f32[8,1,8192]{2,1,0:T(1,128)S(1)}, u32[]{:S(2)}, u32[]{:S(2)}) %all-to-all-start.2) | async-done | bytes 262176 | tf_op jit(solution)/shard_map/all_to_all | solution.py:66
  198.7 0.9 fusion.12
  (136 shorter events, 7.4 us)
Async XLA Ops:
  0.0 74.0 %copy-start = (bf16[2,96,2048]{2,1,0:T(8,128)(2,1)S(1)}, bf16[2,96,2048]{2,1,0:T(8,128)(2,1)}, u32[]{:S(2)}) copy-start(bf16[2,96,2048]{2,1,0:T(8,128)(2,1)} %param.7) | copy-start | bytes 2359300
  0.0 29.9 %copy-start.1 = (s32[8]{0:T(128)S(1)}, s32[8]{0:T(128)}, u32[]{:S(2)}) copy-start(s32[8]{0:T(128)} %constant.142) | copy-start | bytes 100
  0.0 30.7 %copy-start.2 = (bf16[2,96,2048]{2,1,0:T(8,128)(2,1)S(1)}, bf16[2,96,2048]{2,1,0:T(8,128)(2,1)}, u32[]{:S(2)}) copy-start(bf16[2,96,2048]{2,1,0:T(8,128)(2,1)} %param.9) | copy-start | bytes 2359300
  1.0 30.6 %collective-permute-start = (bf16[32,1024]{1,0:T(8,128)(2,1)S(1)}, bf16[32,1024]{1,0:T(8,128)(2,1)S(1)}, u32[]{:S(2)}, u32[]{:S(2)}) collective-permute-start(bf16[32,1024]{1,0:T(8,128)(2,1)S(1)} %get-tuple-element.12), channel_id=1, source_target_pairs={{0,1},{1,2},{2,3},{3,4},{4,5},{5,6},{6,7},{7,16},{8,9},{9,10},{10,... | collective-permute-start | bytes 196616 | tf_op jit(solution)/shard_map/ppermute | solution.py:27
  4.8 31.4 %collective-permute-start.1 = (bf16[32,1024]{1,0:T(8,128)(2,1)S(1)}, bf16[32,1024]{1,0:T(8,128)(2,1)S(1)}, u32[]{:S(2)}, u32[]{:S(2)}) collective-permute-start(bf16[32,1024]{1,0:T(8,128)(2,1)S(1)} %get-tuple-element.12), channel_id=1, source_target_pairs={{0,2},{1,3},{2,4},{3,5},{4,6},{5,7},{6,16},{7,17},{8,10},{9,11},{1... | collective-permute-start | bytes 196616 | tf_op jit(solution)/shard_map/ppermute | solution.py:27
  11.2 27.0 %collective-permute-start.2 = (bf16[32,1024]{1,0:T(8,128)(2,1)S(1)}, bf16[32,1024]{1,0:T(8,128)(2,1)S(1)}, u32[]{:S(2)}, u32[]{:S(2)}) collective-permute-start(bf16[32,1024]{1,0:T(8,128)(2,1)S(1)} %get-tuple-element.12), channel_id=1, source_target_pairs={{0,3},{1,4},{2,5},{3,6},{4,7},{5,16},{6,17},{7,18},{8,11},{9,12},{... | collective-permute-start | bytes 196616 | tf_op jit(solution)/shard_map/ppermute | solution.py:27
  17.8 23.8 %collective-permute-start.3 = (bf16[32,1024]{1,0:T(8,128)(2,1)S(1)}, bf16[32,1024]{1,0:T(8,128)(2,1)S(1)}, u32[]{:S(2)}, u32[]{:S(2)}) collective-permute-start(bf16[32,1024]{1,0:T(8,128)(2,1)S(1)} %get-tuple-element.12), channel_id=1, source_target_pairs={{0,4},{1,5},{2,6},{3,7},{4,16},{5,17},{6,18},{7,19},{8,12},{9,13},... | collective-permute-start | bytes 196616 | tf_op jit(solution)/shard_map/ppermute | solution.py:27
  24.2 23.5 %collective-permute-start.4 = (bf16[32,1024]{1,0:T(8,128)(2,1)S(1)}, bf16[32,1024]{1,0:T(8,128)(2,1)S(1)}, u32[]{:S(2)}, u32[]{:S(2)}) collective-permute-start(bf16[32,1024]{1,0:T(8,128)(2,1)S(1)} %get-tuple-element.12), channel_id=1, source_target_pairs={{0,23},{1,0},{2,1},{3,2},{4,3},{5,4},{6,5},{7,6},{8,31},{9,8},{10,... | collective-permute-start | bytes 196616 | tf_op jit(solution)/shard_map/ppermute | solution.py:27
  31.7 18.7 %collective-permute-start.5 = (bf16[32,1024]{1,0:T(8,128)(2,1)S(1)}, bf16[32,1024]{1,0:T(8,128)(2,1)S(1)}, u32[]{:S(2)}, u32[]{:S(2)}) collective-permute-start(bf16[32,1024]{1,0:T(8,128)(2,1)S(1)} %get-tuple-element.12), channel_id=1, source_target_pairs={{0,22},{1,23},{2,0},{3,1},{4,2},{5,3},{6,4},{7,5},{8,30},{9,31},{1... | collective-permute-start | bytes 196616 | tf_op jit(solution)/shard_map/ppermute | solution.py:27
  36.3 19.5 %collective-permute-start.6 = (bf16[32,1024]{1,0:T(8,128)(2,1)S(1)}, bf16[32,1024]{1,0:T(8,128)(2,1)S(1)}, u32[]{:S(2)}, u32[]{:S(2)}) collective-permute-start(bf16[32,1024]{1,0:T(8,128)(2,1)S(1)} %get-tuple-element.12), channel_id=1, source_target_pairs={{0,21},{1,22},{2,23},{3,0},{4,1},{5,2},{6,3},{7,4},{8,29},{9,30},{... | collective-permute-start | bytes 196616 | tf_op jit(solution)/shard_map/ppermute | solution.py:27
  38.2 24.1 %collective-permute-start.11 = (bf16[2,96,256]{2,1,0:T(8,128)(2,1)}, bf16[2,96,256]{2,1,0:T(8,128)(2,1)S(1)}, u32[]{:S(2)}, u32[]{:S(2)}) collective-permute-start(bf16[2,96,256]{2,1,0:T(8,128)(2,1)} %get-tuple-element.20), channel_id=1, source_target_pairs={{0,1},{1,2},{2,3},{3,4},{4,5},{5,6},{6,7},{7,0},{8,9},{9,10},{10,1... | collective-permute-start | bytes 294920 | tf_op jit(solution)/shard_map/ppermute | solution.py:55
  41.6 22.7 %collective-permute-start.12 = (bf16[2,96,256]{2,1,0:T(8,128)(2,1)}, bf16[2,96,256]{2,1,0:T(8,128)(2,1)S(1)}, u32[]{:S(2)}, u32[]{:S(2)}) collective-permute-start(bf16[2,96,256]{2,1,0:T(8,128)(2,1)} %get-tuple-element.19), channel_id=1, source_target_pairs={{0,2},{1,3},{2,4},{3,5},{4,6},{5,7},{6,0},{7,1},{8,10},{9,11},{10,... | collective-permute-start | bytes 294920 | tf_op jit(solution)/shard_map/ppermute | solution.py:55
  47.7 20.1 %collective-permute-start.13 = (bf16[2,96,256]{2,1,0:T(8,128)(2,1)}, bf16[2,96,256]{2,1,0:T(8,128)(2,1)S(1)}, u32[]{:S(2)}, u32[]{:S(2)}) collective-permute-start(bf16[2,96,256]{2,1,0:T(8,128)(2,1)} %get-tuple-element.18), channel_id=1, source_target_pairs={{0,3},{1,4},{2,5},{3,6},{4,7},{5,0},{6,1},{7,2},{8,11},{9,12},{10,... | collective-permute-start | bytes 294920 | tf_op jit(solution)/shard_map/ppermute | solution.py:55
  50.3 27.8 %collective-permute-start.14 = (bf16[2,96,256]{2,1,0:T(8,128)(2,1)}, bf16[2,96,256]{2,1,0:T(8,128)(2,1)S(1)}, u32[]{:S(2)}, u32[]{:S(2)}) collective-permute-start(bf16[2,96,256]{2,1,0:T(8,128)(2,1)} %get-tuple-element.17), channel_id=1, source_target_pairs={{0,4},{1,5},{2,6},{3,7},{4,0},{5,1},{6,2},{7,3},{8,12},{9,13},{10,... | collective-permute-start | bytes 294920 | tf_op jit(solution)/shard_map/ppermute | solution.py:55
  55.7 34.7 %collective-permute-start.15 = (bf16[2,96,256]{2,1,0:T(8,128)(2,1)}, bf16[2,96,256]{2,1,0:T(8,128)(2,1)S(1)}, u32[]{:S(2)}, u32[]{:S(2)}) collective-permute-start(bf16[2,96,256]{2,1,0:T(8,128)(2,1)} %get-tuple-element.16), channel_id=1, source_target_pairs={{0,5},{1,6},{2,7},{3,0},{4,1},{5,2},{6,3},{7,4},{8,13},{9,14},{10,... | collective-permute-start | bytes 294920 | tf_op jit(solution)/shard_map/ppermute | solution.py:55
  62.2 2.1 %copy-start.3 = (bf16[2,96,256]{2,1,0:T(8,128)(2,1)S(1)}, bf16[2,96,256]{2,1,0:T(8,128)(2,1)}, u32[]{:S(2)}) copy-start(bf16[2,96,256]{2,1,0:T(8,128)(2,1)} %get-tuple-element.21) | copy-start | bytes 294916
  62.3 11.5 %collective-permute-start.7 = (bf16[256,1024]{1,0:T(8,128)(2,1)S(1)}, bf16[256,1024]{1,0:T(8,128)(2,1)S(1)}, u32[]{:S(2)}, u32[]{:S(2)}) collective-permute-start(bf16[256,1024]{1,0:T(8,128)(2,1)S(1)} %bitcast_select_fusion), channel_id=1, source_target_pairs={{0,8},{8,0},{16,24},{24,16},{32,40},{40,32},{48,56},{56,48},{64,72... | collective-permute-start | bytes 1572872 | tf_op jit(solution)/shard_map/ppermute | solution.py:81
  64.3 40.4 %collective-permute-start.16 = (bf16[2,96,256]{2,1,0:T(8,128)(2,1)S(1)}, bf16[2,96,256]{2,1,0:T(8,128)(2,1)S(1)}, u32[]{:S(2)}, u32[]{:S(2)}) collective-permute-start(bf16[2,96,256]{2,1,0:T(8,128)(2,1)S(1)} %copy-done.3), channel_id=1, source_target_pairs={{0,6},{1,7},{2,0},{3,1},{4,2},{5,3},{6,4},{7,5},{8,14},{9,15},{10,... | collective-permute-start | bytes 294920 | tf_op jit(solution)/shard_map/ppermute | solution.py:55
  67.8 36.9 %collective-permute-start.17 = (bf16[2,96,256]{2,1,0:T(8,128)(2,1)S(1)}, bf16[2,96,256]{2,1,0:T(8,128)(2,1)S(1)}, u32[]{:S(2)}, u32[]{:S(2)}) collective-permute-start(bf16[2,96,256]{2,1,0:T(8,128)(2,1)S(1)} %get-tuple-element.15), channel_id=1, source_target_pairs={{0,7},{1,0},{2,1},{3,2},{4,3},{5,4},{6,5},{7,6},{8,15},{9,8},{10,9... | collective-permute-start | bytes 294920 | tf_op jit(solution)/shard_map/ppermute | solution.py:55
  74.1 1.1 copy-start.4
  75.7 11.7 %collective-permute-start.8 = (bf16[1,2,256,96]{2,3,1,0:T(8,128)(2,1)S(1)}, bf16[1,2,256,96]{2,3,1,0:T(8,128)(2,1)S(1)}, u32[]{:S(2)}, u32[]{:S(2)}) collective-permute-start(bf16[1,2,256,96]{2,3,1,0:T(8,128)(2,1)S(1)} %fusion.3), channel_id=1, source_target_pairs={{0,4},{1,5},{2,6},{3,7},{4,0},{5,1},{6,2},{7,3},{8,12},{9,13},{10,... | collective-permute-start | bytes 294920 | tf_op jit(solution)/shard_map/ppermute | solution.py:41
  87.4 11.6 %collective-permute-start.9 = (bf16[2,2,256,96]{2,3,1,0:T(8,128)(2,1)S(1)}, bf16[2,2,256,96]{2,3,1,0:T(8,128)(2,1)S(1)}, u32[]{:S(2)}, u32[]{:S(2)}) collective-permute-start(bf16[2,2,256,96]{2,3,1,0:T(8,128)(2,1)S(1)} %pad_maximum_fusion.2), channel_id=1, source_target_pairs={{0,2},{1,3},{2,0},{3,1},{4,6},{5,7},{6,4},{7,5},{8,10},{9,11},{10,... | collective-permute-start | bytes 589832 | tf_op jit(solution)/shard_map/ppermute | solution.py:41
  99.1 14.9 %collective-permute-start.10 = (bf16[4,2,256,96]{2,3,1,0:T(8,128)(2,1)S(1)}, bf16[4,2,256,96]{2,3,1,0:T(8,128)(2,1)}, u32[]{:S(2)}, u32[]{:S(2)}) collective-permute-start(bf16[4,2,256,96]{2,3,1,0:T(8,128)(2,1)S(1)} %pad_maximum_fusion.1), channel_id=1, source_target_pairs={{0,1},{1,0},{2,3},{3,2},{4,5},{5,4},{6,7},{7,6},{8,9},{9,8},{10,11... | collective-permute-start | bytes 1179656 | tf_op jit(solution)/shard_map/ppermute | solution.py:41
  177.1 21.4 %all-to-all-start.2 = ((f32[8,1,8192]{2,1,0:T(1,128)}), f32[8,1,8192]{2,1,0:T(1,128)S(1)}, u32[]{:S(2)}, u32[]{:S(2)}) async-start(f32[8,1,8192]{2,1,0:T(1,128)} %broadcast_in_dim.74), calls=%async_computation.2 | async-start | bytes 524288 | tf_op jit(solution)/shard_map/all_to_all | solution.py:66
